TPU v7x, 512 devices: a whole 4x4x16 slice. The times are simulated.
512 devices in a mesh: xb: 16 (over x, y), zs: 32 (over z, core).
Axes of the slice: x: 4, y: 4, z: 16, core: 2. Of those that a mesh axis runs over, the one named last changes fastest.
Arguments:
- partials: bfloat16 [16384, 32768], P(('xb', 'zs')), may hold values from -6 to 6
- routes: int32 [512, 32], P(('xb', 'zs')), may hold values from 0 to 255, as said below
- taps: float32 [3, 129], replicated, may hold values from 0.25 to 2.5
Outputs:
- gradient: float32 [1024, 1024, 128], P('xb', 'zs')
- smoothed: float32 [1024, 1024, 128], P('xb', 'zs')
Inputs may be any that keep to these rules, and one draw needn't show every extreme that they name: `routes`: an entry v of a device's list names local block v % (8) of the device with zs index v // 8 in the same xb group; the entries of one list that name the same owner all name the same block, and no owner is named by more than two entries of one list.
All inputs are finite; a program needn't handle non-finite values.
Results may differ from a plain program's by a relative error of at most 0.0077.
Values may be sent and summed in bfloat16 or wider, within the bound.
No kernel may reach another device: no remote copies, remote signals or barrier semaphores. Data moves between devices by JAX's collectives and lax.ppermute only.
A program may use at most 64 MiB of HBM per device.

v0:
```python
import jax
import jax.numpy as jnp
from jax import lax
from jax.sharding import PartitionSpec as P

BLK = 32
YBLOCKS = 4
CELLS = 32768
CX = 64
CZ = 32
REACH = 64
NY = 128


def extended_2(x, sides, width):
    for axis, dim in sides:
        count, length = (lax.axis_size(axis), x.shape[dim])
        up = [(i, (i + 1) % count) for i in range(count - 1)]
        down = [(j, i) for i, j in up]
        last = lax.slice_in_dim(x, length - width, length, axis=dim)
        initial = lax.slice_in_dim(x, 0, width, axis=dim)
        before = lax.ppermute(last, axis, up)
        after = lax.ppermute(initial, axis, down)
        x = jnp.concatenate([before, x, after], axis=dim)
    return x


def band_matrix(kern_row, rows, cols, offset):
    border = rows + cols
    widened = jnp.pad(kern_row, ((border, border),))
    front = widened[offset + border : offset + border + cols]
    behind = widened[offset + border - rows : offset + border]
    cycle = jnp.concatenate([front, behind])
    period = rows + cols - 1
    tiled = jnp.tile(cycle, rows)[: rows * period]
    return tiled.reshape(rows, period)[:, :cols]


def body(partials, routes, taps):
    owners_count = lax.axis_size("zs")
    blocks_local = 2 * YBLOCKS
    entries = routes[0]
    owner = entries // blocks_local
    block_id = entries % blocks_local
    owner_hit = owner[:, None] == jnp.arange(owners_count)[None, :]
    hit_count = owner_hit.astype(jnp.int32)
    earlier = jnp.cumsum(hit_count, axis=0) - hit_count
    rank = jnp.sum(earlier * hit_count, axis=1)
    target = owner * 2 + rank
    select = target[None, :] == jnp.arange(2 * owners_count)[:, None]
    packed = jnp.dot(select.astype(jnp.bfloat16), partials, preferred_element_type=jnp.float32)
    packed = packed.astype(jnp.bfloat16).reshape(owners_count, 2, CELLS)
    packed_ids = jnp.sum(jnp.where(select, block_id[None, :], 0), axis=1).reshape(owners_count, 2)
    arrived, arrived_ids = (
        lax.all_to_all(packed, "zs", split_axis=0, concat_axis=0, tiled=True),
        lax.all_to_all(packed_ids, "zs", split_axis=0, concat_axis=0, tiled=True),
    )
    contrib = (arrived[:, 0].astype(jnp.float32) + arrived[:, 1].astype(jnp.float32)).astype(
        jnp.bfloat16
    )
    source_ids = arrived_ids[:, 0]
    placing = (source_ids[None, :] == jnp.arange(blocks_local)[:, None]).astype(jnp.bfloat16)
    assembled = jnp.dot(placing, contrib, preferred_element_type=jnp.float32)
    assembled = assembled.reshape(2, YBLOCKS, BLK, BLK, BLK).transpose(0, 2, 4, 1, 3)
    gradient = assembled.reshape(CX, CZ, NY)
    norms = jnp.sqrt(jnp.sum(taps * taps, axis=1, keepdims=True))
    kernel = (taps / norms).astype(jnp.bfloat16)
    field = gradient.astype(jnp.bfloat16)
    padded = extended_2(field, (("xb", 0),), CX)
    x_matrix = band_matrix(kernel[0], CX, 3 * CX, 0)
    along_x = jnp.dot(x_matrix, padded.reshape(3 * CX, CZ * NY), preferred_element_type=jnp.float32)
    along_x = along_x.astype(jnp.bfloat16).reshape(CX, CZ, NY)
    y_matrix = band_matrix(kernel[1], NY, NY, REACH)
    along_y = jnp.einsum(
        "ab,xzb->xza", y_matrix, along_x, preferred_element_type=jnp.float32
    ).astype(jnp.bfloat16)
    line_length = CZ * owners_count
    columns = CX * NY // owners_count
    z_major = along_y.transpose(1, 0, 2).reshape(CZ, owners_count, columns)
    z_matrix = band_matrix(kernel[2], REACH, 3 * REACH, 0)
    lines = lax.all_to_all(z_major, "zs", split_axis=1, concat_axis=0, tiled=True)
    flat = lines.reshape(line_length, lines.shape[2])
    extended = jnp.pad(flat, ((REACH, REACH), (0, 0)))
    pieces = extended.reshape(line_length // REACH + 2, REACH, flat.shape[1])
    windows = jnp.concatenate([pieces[:-2], pieces[1:-1], pieces[2:]], axis=1)
    filtered = jnp.einsum("ij,bjm->bim", z_matrix, windows, preferred_element_type=jnp.float32)
    filtered = filtered.reshape(line_length, 1, flat.shape[1])
    returned = lax.all_to_all(filtered, "zs", split_axis=0, concat_axis=1, tiled=True)
    smoothed = returned.reshape(CZ, CX, NY).transpose(1, 0, 2)
    return (gradient, smoothed)


def solution(mesh):
    placed = (P(("xb", "zs"), None), P(("xb", "zs"), None), P())
    return jax.shard_map(
        body,
        mesh=mesh,
        in_specs=placed,
        out_specs=(P("xb", "zs", None), P("xb", "zs", None)),
        check_vma=False,
    )
```

profile of v0, /device:TPU:26, one launch (start us, length us, event | category | flops | bytes accessed | tf_op | source)
XLA Modules:
  0.0 409.5 jit_solution(13148397627251615303)
XLA Ops:
  3.3 15.5 %all-to-all-start = ((s32[32,1,2]{2,1,0:T(1,128)}), s32[32,1,2]{2,1,0:T(1,128)S(1)}, u32[]{:S(2)}, u32[]{:S(2)}) async-start(s32[32,1,2]{2,1,0:T(1,128)} %bitcast.4), calls=%async_computation | async-start | bytes 32768 | tf_op jit(solution)/shard_map/all_to_all | solution.py:56
  18.8 3.3 convolution_convert_fusion
  22.1 7.6 %reshape.109 = bf16[32,2,32768]{2,1,0:T(2,128)(2,1)} reshape(bf16[64,32768]{1,0:T(8,128)(2,1)} %convolution_convert_fusion) | data formatting | bytes 8388608 | tf_op jit(solution)/shard_map/reshape | solution.py:52
  29.7 1.4 all-to-all-done
  31.1 11.2 %all-to-all-start.1 = ((bf16[32,2,32768]{2,1,0:T(2,128)(2,1)}), bf16[32,2,32768]{2,1,0:T(2,128)(2,1)}, u32[]{:S(2)}, u32[]{:S(2)}) async-start(bf16[32,2,32768]{2,1,0:T(2,128)(2,1)} %reshape.109), calls=%async_computation.1 | async-start | bytes 8388608 | tf_op jit(solution)/shard_map/all_to_all | solution.py:55
  42.7 183.2 %all-to-all-done.1 = bf16[32,2,32768]{2,1,0:T(2,128)(2,1)} async-done(((bf16[32,2,32768]{2,1,0:T(2,128)(2,1)}), bf16[32,2,32768]{2,1,0:T(2,128)(2,1)}, u32[]{:S(2)}, u32[]{:S(2)}) %all-to-all-start.1) | async-done | bytes 4194336 | tf_op jit(solution)/shard_map/all_to_all | solution.py:55
  225.9 9.0 %fusion.23 = (bf16[32,1,32768]{2,1,0:T(2,128)(2,1)S(1)}, bf16[32,1,32768]{2,1,0:T(2,128)(2,1)S(1)}) fusion(bf16[32,2,32768]{2,1,0:T(2,128)(2,1)} %all-to-all-done.1), kind=kLoop, calls=%fused_computation.61 | loop fusion | bytes 8388608 | tf_op jit(solution)/shard_map/slice | solution.py:58
  234.9 5.9 %fusion = bf16[32768,32]{0,1:T(8,128)(2,1)} fusion(bf16[32,1,32768]{2,1,0:T(2,128)(2,1)S(1)} %get-tuple-element.14, bf16[32,1,32768]{2,1,0:T(2,128)(2,1)S(1)} %get-tuple-element.13), kind=kLoop, calls=%fused_computation.4 | loop fusion | flops 4194304 | bytes 6291456 | tf_op jit(solution)/shard_map/dot_general | solution.py:63
  240.8 7.4 %copy.46 = bf16[32768,32]{1,0:T(8,128)(2,1)} copy(bf16[32768,32]{0,1:T(8,128)(2,1)} %fusion) | data formatting | bytes 4194304 | tf_op jit(solution)/shard_map/dot_general | solution.py:63
  248.1 16.3 %convolution_bitcast_fusion = f32[2,32,32,4,32]{2,3,4,1,0:T(4,128)} fusion(bf16[32,32,32,32,1]{3,2,1,0,4:T(8,128)(2,1)} %bitcast.86, s32[2,4]{1,0:T(2,128)S(1)} %multiply_add_fusion, s32[32]{0:T(128)S(1)} %slice_bitcast_fusion.4), kind=kOutput, calls=%fused_computation.3 | convolution fusion | flops 16777472 | bytes 3145888 | tf_op jit(solution)/shard_map/dot_general | solution.py:63
  264.4 6.3 %copy.39 = f32[2,32,32,4,32]{4,3,2,1,0:T(4,128)} copy(f32[2,32,32,4,32]{2,3,4,1,0:T(4,128)} %convolution_bitcast_fusion) | data formatting | bytes 2097152 | tf_op jit(solution)/shard_map/transpose | solution.py:64
  270.7 3.7 reshape.110
  275.5 3.0 collective-permute-start
  278.5 3.0 collective-permute-start.1
  282.3 8.9 %collective-permute-done = bf16[64,32,128]{2,1,0:T(8,128)(2,1)} collective-permute-done((bf16[64,32,128]{2,1,0:T(8,128)(2,1)}, bf16[64,32,128]{2,1,0:T(8,128)(2,1)}, u32[]{:S(2)}, u32[]{:S(2)}) %collective-permute-start) | collective-permute-done | bytes 524320 | tf_op jit(solution)/shard_map/ppermute | solution.py:22
  291.2 4.9 %collective-permute-done.1 = bf16[64,32,128]{2,1,0:T(8,128)(2,1)} collective-permute-done((bf16[64,32,128]{2,1,0:T(8,128)(2,1)}, bf16[64,32,128]{2,1,0:T(8,128)(2,1)}, u32[]{:S(2)}, u32[]{:S(2)}) %collective-permute-start.1) | collective-permute-done | bytes 524320 | tf_op jit(solution)/shard_map/ppermute | solution.py:23
  296.1 1.5 pad_maximum_fusion
  299.1 1.1 copy.41
  300.1 9.9 %all-to-all-start.2 = ((bf16[32,32,256]{2,0,1:T(8,128)(2,1)}), bf16[32,32,256]{2,0,1:T(8,128)(2,1)S(1)}, u32[]{:S(2)}, u32[]{:S(2)}) async-start(bf16[32,32,256]{2,0,1:T(8,128)(2,1)} %copy.41), calls=%async_computation.2 | async-start | bytes 1048576 | tf_op jit(solution)/shard_map/all_to_all | solution.py:81
  310.3 33.5 %all-to-all-done.2 = bf16[32,32,256]{2,0,1:T(8,128)(2,1)S(1)} async-done(((bf16[32,32,256]{2,0,1:T(8,128)(2,1)}), bf16[32,32,256]{2,0,1:T(8,128)(2,1)S(1)}, u32[]{:S(2)}, u32[]{:S(2)}) %all-to-all-start.2) | async-done | bytes 524320 | tf_op jit(solution)/shard_map/all_to_all | solution.py:81
  344.3 1.1 copy.42
  345.4 59.5 %all_to_all.47 = f32[1024,1,256]{2,1,0:T(1,128)S(1)} all-to-all(f32[1024,1,256]{2,1,0:T(1,128)S(1)} %copy.42), channel_id=1, replica_groups=mesh['xb'=16,'zs'=32] {'zs'}, dimensions={0} | all-to-all | bytes 2097152 | tf_op jit(solution)/shard_map/all_to_all | solution.py:88
  405.6 1.1 reshape.119
  406.7 2.8 copy.44
  (44 shorter events, 7.5 us)
Async XLA Ops:
  0.6 18.1 %copy-start = (bf16[32,32768]{1,0:T(8,128)(2,1)S(1)}, bf16[32,32768]{1,0:T(8,128)(2,1)}, u32[]{:S(2)}) copy-start(bf16[32,32768]{1,0:T(8,128)(2,1)} %param.3) | copy-start | bytes 6291460
  3.3 27.9 %all-to-all-start = ((s32[32,1,2]{2,1,0:T(1,128)}), s32[32,1,2]{2,1,0:T(1,128)S(1)}, u32[]{:S(2)}, u32[]{:S(2)}) async-start(s32[32,1,2]{2,1,0:T(1,128)} %bitcast.4), calls=%async_computation | async-start | bytes 32768 | tf_op jit(solution)/shard_map/all_to_all | solution.py:56
  29.7 12.6 %copy-start.2 = (f32[3,129]{1,0:T(4,128)S(1)}, f32[3,129]{1,0:T(4,128)}, u32[]{:S(2)}) copy-start(f32[3,129]{1,0:T(4,128)} %param.5) | copy-start | bytes 4648
  31.1 194.8 %all-to-all-start.1 = ((bf16[32,2,32768]{2,1,0:T(2,128)(2,1)}), bf16[32,2,32768]{2,1,0:T(2,128)(2,1)}, u32[]{:S(2)}, u32[]{:S(2)}) async-start(bf16[32,2,32768]{2,1,0:T(2,128)(2,1)} %reshape.109), calls=%async_computation.1 | async-start | bytes 8388608 | tf_op jit(solution)/shard_map/all_to_all | solution.py:55
  274.4 23.8 %copy-start.1 = (f32[64,32,128]{2,1,0:T(8,128)}, f32[64,32,128]{2,1,0:T(8,128)S(1)}, u32[]{:S(2)}) copy-start(f32[64,32,128]{2,1,0:T(8,128)S(1)} %reshape.110) | copy-start | bytes 3145732
  275.5 15.7 %collective-permute-start = (bf16[64,32,128]{2,1,0:T(8,128)(2,1)}, bf16[64,32,128]{2,1,0:T(8,128)(2,1)}, u32[]{:S(2)}, u32[]{:S(2)}) collective-permute-start(bf16[64,32,128]{2,1,0:T(8,128)(2,1)} %convert_element_type.51), channel_id=1, source_target_pairs={{0,32},{32,64},{64,96},{96,128},{128,160},{160,192},{192,224},{224... | collective-permute-start | bytes 1572872 | tf_op jit(solution)/shard_map/ppermute | solution.py:22
  278.5 17.5 %collective-permute-start.1 = (bf16[64,32,128]{2,1,0:T(8,128)(2,1)}, bf16[64,32,128]{2,1,0:T(8,128)(2,1)}, u32[]{:S(2)}, u32[]{:S(2)}) collective-permute-start(bf16[64,32,128]{2,1,0:T(8,128)(2,1)} %convert_element_type.51), channel_id=1, source_target_pairs={{32,0},{64,32},{96,64},{128,96},{160,128},{192,160},{224,192},{256... | collective-permute-start | bytes 1572872 | tf_op jit(solution)/shard_map/ppermute | solution.py:23
  300.1 43.7 %all-to-all-start.2 = ((bf16[32,32,256]{2,0,1:T(8,128)(2,1)}), bf16[32,32,256]{2,0,1:T(8,128)(2,1)S(1)}, u32[]{:S(2)}, u32[]{:S(2)}) async-start(bf16[32,32,256]{2,0,1:T(8,128)(2,1)} %copy.41), calls=%async_computation.2 | async-start | bytes 1048576 | tf_op jit(solution)/shard_map/all_to_all | solution.py:81
where the time goes:
time: 410 us; the launch traced here: 409 us
  waiting for transfers between devices  232 us (57%)
  blocking collectives  59.5 us (15%)
  local copies, waits for them, and re-layouts  43 us (10%)
  starting transfers between devices  42.7 us (10%)
  matrix products  21 us (5%)
  other arithmetic  10.5 us (3%)
    all_to_all x1, waiting for transfers between devices, body(): lax.all_to_all(packed, 'zs', split_axis=0, concat_axis=0, tiled=True)  183 us
    all_to_all x1, blocking collectives, body(): lax.all_to_all(filtered, 'zs', split_axis=0, concat_axis=1, tiled=True)  59.5 us
    all_to_all x1, waiting for transfers between devices, body(): lax.all_to_all(z_major, 'zs', split_axis=1, concat_axis=0, tiled=True)  33.5 us
    dot_general x1, matrix products, body(): assembled = jnp.dot(placing, contrib, preferred_element_type=jnp.float32)  16.3 us
    all_to_all x1, starting transfers between devices, body(): lax.all_to_all(packed_ids, 'zs', split_axis=0, concat_axis=0, tiled=True)  15.5 us
    all_to_all x1, starting transfers between devices, body(): lax.all_to_all(packed, 'zs', split_axis=0, concat_axis=0, tiled=True)  11.2 us
    all_to_all x1, starting transfers between devices, body(): lax.all_to_all(z_major, 'zs', split_axis=1, concat_axis=0, tiled=True)  9.94 us
    slice x1, local copies, waits for them, and re-layouts, body(): arrived[:, 0].astype(jnp.float32) + arrived[:, 1].astype(jnp.float32)  8.97 us
  transfers between devices with their start and end apart: 5, of which 5 were waited for; matrix products, arithmetic and copies ran while one was open for 3% of the time, Pallas kernels for 0%

commit v1 on v0

--- a/solution.py
+++ b/solution.py
@@ -85,7 +85,10 @@
     windows = jnp.concatenate([pieces[:-2], pieces[1:-1], pieces[2:]], axis=1)
     filtered = jnp.einsum("ij,bjm->bim", z_matrix, windows, preferred_element_type=jnp.float32)
     filtered = filtered.reshape(line_length, 1, flat.shape[1])
-    returned = lax.all_to_all(filtered, "zs", split_axis=0, concat_axis=1, tiled=True)
+    returned = jnp.concatenate(
+        lax.all_to_all(jnp.stack(jnp.split(filtered, lax.axis_size("zs"), axis=0)), "zs", 0, 0),
+        axis=1,
+    )
     smoothed = returned.reshape(CZ, CX, NY).transpose(1, 0, 2)
     return (gradient, smoothed)
 

time: 410 us -> 410 us (level)
  no operation moved by 1% of the time
where the time goes in v1:
time: 410 us; the launch traced here: 409 us
  waiting for transfers between devices  232 us (57%)
  blocking collectives  59.5 us (15%)
  starting transfers between devices  42.7 us (10%)
  local copies, waits for them, and re-layouts  42 us (10%)
  matrix products  21 us (5%)
  other arithmetic  10.5 us (3%)
    all_to_all x1, waiting for transfers between devices, body(): lax.all_to_all(packed, 'zs', split_axis=0, concat_axis=0, tiled=True)  183 us
    all_to_all x1, blocking collectives, body(): lax.all_to_all(jnp.stack(jnp.split(filtered, lax.axis_size('zs'), axis=0)...  59.5 us
    all_to_all x1, waiting for transfers between devices, body(): lax.all_to_all(z_major, 'zs', split_axis=1, concat_axis=0, tiled=True)  33.5 us
    dot_general x1, matrix products, body(): assembled = jnp.dot(placing, contrib, preferred_element_type=jnp.float32)  16.3 us
    all_to_all x1, starting transfers between devices, body(): lax.all_to_all(packed_ids, 'zs', split_axis=0, concat_axis=0, tiled=True)  15.5 us
    all_to_all x1, starting transfers between devices, body(): lax.all_to_all(packed, 'zs', split_axis=0, concat_axis=0, tiled=True)  11.2 us
    all_to_all x1, starting transfers between devices, body(): lax.all_to_all(z_major, 'zs', split_axis=1, concat_axis=0, tiled=True)  9.94 us
    slice x1, local copies, waits for them, and re-layouts, body(): arrived[:, 0].astype(jnp.float32) + arrived[:, 1].astype(jnp.float32)  8.97 us
  transfers between devices with their start and end apart: 5, of which 5 were waited for; matrix products, arithmetic and copies ran while one was open for 3% of the time, Pallas kernels for 0%

profile of v1, /device:TPU:26, one launch (start us, length us, event | category | flops | bytes accessed | tf_op | source)
XLA Modules:
  0.0 408.8 jit_solution(4977809685706745613)
XLA Ops:
  3.3 15.5 %all-to-all-start = ((s32[32,1,2]{2,1,0:T(1,128)}), s32[32,1,2]{2,1,0:T(1,128)S(1)}, u32[]{:S(2)}, u32[]{:S(2)}) async-start(s32[32,1,2]{2,1,0:T(1,128)} %bitcast.4), calls=%async_computation | async-start | bytes 32768 | tf_op jit(solution)/shard_map/all_to_all | solution.py:56
  18.8 3.3 convolution_convert_fusion
  22.1 7.6 %reshape.108 = bf16[32,2,32768]{2,1,0:T(2,128)(2,1)} reshape(bf16[64,32768]{1,0:T(8,128)(2,1)} %convolution_convert_fusion) | data formatting | bytes 8388608 | tf_op jit(solution)/shard_map/reshape | solution.py:52
  29.7 1.4 all-to-all-done
  31.1 11.2 %all-to-all-start.1 = ((bf16[32,2,32768]{2,1,0:T(2,128)(2,1)}), bf16[32,2,32768]{2,1,0:T(2,128)(2,1)}, u32[]{:S(2)}, u32[]{:S(2)}) async-start(bf16[32,2,32768]{2,1,0:T(2,128)(2,1)} %reshape.108), calls=%async_computation.1 | async-start | bytes 8388608 | tf_op jit(solution)/shard_map/all_to_all | solution.py:55
  42.7 183.2 %all-to-all-done.1 = bf16[32,2,32768]{2,1,0:T(2,128)(2,1)} async-done(((bf16[32,2,32768]{2,1,0:T(2,128)(2,1)}), bf16[32,2,32768]{2,1,0:T(2,128)(2,1)}, u32[]{:S(2)}, u32[]{:S(2)}) %all-to-all-start.1) | async-done | bytes 4194336 | tf_op jit(solution)/shard_map/all_to_all | solution.py:55
  225.9 9.0 %fusion.23 = (bf16[32,1,32768]{2,1,0:T(2,128)(2,1)S(1)}, bf16[32,1,32768]{2,1,0:T(2,128)(2,1)S(1)}) fusion(bf16[32,2,32768]{2,1,0:T(2,128)(2,1)} %all-to-all-done.1), kind=kLoop, calls=%fused_computation.125 | loop fusion | bytes 8388608 | tf_op jit(solution)/shard_map/slice | solution.py:58
  234.9 5.9 %fusion = bf16[32768,32]{0,1:T(8,128)(2,1)} fusion(bf16[32,1,32768]{2,1,0:T(2,128)(2,1)S(1)} %get-tuple-element.14, bf16[32,1,32768]{2,1,0:T(2,128)(2,1)S(1)} %get-tuple-element.13), kind=kLoop, calls=%fused_computation.4 | loop fusion | flops 4194304 | bytes 6291456 | tf_op jit(solution)/shard_map/dot_general | solution.py:63
  240.8 7.4 %copy.107 = bf16[32768,32]{1,0:T(8,128)(2,1)} copy(bf16[32768,32]{0,1:T(8,128)(2,1)} %fusion) | data formatting | bytes 4194304 | tf_op jit(solution)/shard_map/dot_general | solution.py:63
  248.1 16.3 %convolution_bitcast_fusion = f32[2,32,32,4,32]{2,3,4,1,0:T(4,128)} fusion(bf16[32,32,32,32,1]{3,2,1,0,4:T(8,128)(2,1)} %bitcast.212, s32[2,4]{1,0:T(2,128)S(1)} %multiply_add_fusion, s32[32]{0:T(128)S(1)} %slice_bitcast_fusion.36), kind=kOutput, calls=%fused_computation.3 | convolution fusion | flops 16777472 | bytes 3145888 | tf_op jit(solution)/shard_map/dot_general | solution.py:63
  264.4 6.3 %copy.101 = f32[2,32,32,4,32]{4,3,2,1,0:T(4,128)} copy(f32[2,32,32,4,32]{2,3,4,1,0:T(4,128)} %convolution_bitcast_fusion) | data formatting | bytes 2097152 | tf_op jit(solution)/shard_map/transpose | solution.py:64
  270.7 3.7 reshape.109
  274.4 1.0 convert_element_type.51
  275.5 3.0 collective-permute-start
  278.5 3.0 collective-permute-start.1
  282.3 8.9 %collective-permute-done = bf16[64,32,128]{2,1,0:T(8,128)(2,1)} collective-permute-done((bf16[64,32,128]{2,1,0:T(8,128)(2,1)}, bf16[64,32,128]{2,1,0:T(8,128)(2,1)}, u32[]{:S(2)}, u32[]{:S(2)}) %collective-permute-start) | collective-permute-done | bytes 524320 | tf_op jit(solution)/shard_map/ppermute | solution.py:22
  291.2 4.9 %collective-permute-done.1 = bf16[64,32,128]{2,1,0:T(8,128)(2,1)} collective-permute-done((bf16[64,32,128]{2,1,0:T(8,128)(2,1)}, bf16[64,32,128]{2,1,0:T(8,128)(2,1)}, u32[]{:S(2)}, u32[]{:S(2)}) %collective-permute-start.1) | collective-permute-done | bytes 524320 | tf_op jit(solution)/shard_map/ppermute | solution.py:23
  296.1 1.5 pad_maximum_fusion
  299.1 1.1 copy.103
  300.1 9.9 %all-to-all-start.2 = ((bf16[32,32,256]{2,0,1:T(8,128)(2,1)}), bf16[32,32,256]{2,0,1:T(8,128)(2,1)S(1)}, u32[]{:S(2)}, u32[]{:S(2)}) async-start(bf16[32,32,256]{2,0,1:T(8,128)(2,1)} %copy.103), calls=%async_computation.2 | async-start | bytes 1048576 | tf_op jit(solution)/shard_map/all_to_all | solution.py:81
  310.3 33.5 %all-to-all-done.2 = bf16[32,32,256]{2,0,1:T(8,128)(2,1)S(1)} async-done(((bf16[32,32,256]{2,0,1:T(8,128)(2,1)}), bf16[32,32,256]{2,0,1:T(8,128)(2,1)S(1)}, u32[]{:S(2)}, u32[]{:S(2)}) %all-to-all-start.2) | async-done | bytes 524320 | tf_op jit(solution)/shard_map/all_to_all | solution.py:81
  344.8 59.5 %all_to_all.37 = f32[32,32,1,256]{3,1,2,0:T(8,128)S(1)} all-to-all(f32[32,32,1,256]{3,1,2,0:T(8,128)S(1)} %constant_dynamic-update-slice_fusion), channel_id=1, replica_groups=mesh['xb'=16,'zs'=32] {'zs'}, dimensions={0} | all-to-all | bytes 2097152 | tf_op jit(solution)/shard_map/all_to_all | solution.py:89
  404.9 1.1 reshape_reshape.3
  405.9 2.8 copy.105
  (74 shorter events, 6.5 us)
Async XLA Ops:
  0.6 18.1 %copy-start = (bf16[32,32768]{1,0:T(8,128)(2,1)S(1)}, bf16[32,32768]{1,0:T(8,128)(2,1)}, u32[]{:S(2)}) copy-start(bf16[32,32768]{1,0:T(8,128)(2,1)} %param.3) | copy-start | bytes 6291460
  3.3 27.9 %all-to-all-start = ((s32[32,1,2]{2,1,0:T(1,128)}), s32[32,1,2]{2,1,0:T(1,128)S(1)}, u32[]{:S(2)}, u32[]{:S(2)}) async-start(s32[32,1,2]{2,1,0:T(1,128)} %bitcast.4), calls=%async_computation | async-start | bytes 32768 | tf_op jit(solution)/shard_map/all_to_all | solution.py:56
  29.7 12.6 %copy-start.2 = (f32[3,129]{1,0:T(4,128)S(1)}, f32[3,129]{1,0:T(4,128)}, u32[]{:S(2)}) copy-start(f32[3,129]{1,0:T(4,128)} %param.5) | copy-start | bytes 4648
  31.1 194.8 %all-to-all-start.1 = ((bf16[32,2,32768]{2,1,0:T(2,128)(2,1)}), bf16[32,2,32768]{2,1,0:T(2,128)(2,1)}, u32[]{:S(2)}, u32[]{:S(2)}) async-start(bf16[32,2,32768]{2,1,0:T(2,128)(2,1)} %reshape.108), calls=%async_computation.1 | async-start | bytes 8388608 | tf_op jit(solution)/shard_map/all_to_all | solution.py:55
  274.4 23.8 %copy-start.1 = (f32[64,32,128]{2,1,0:T(8,128)}, f32[64,32,128]{2,1,0:T(8,128)S(1)}, u32[]{:S(2)}) copy-start(f32[64,32,128]{2,1,0:T(8,128)S(1)} %reshape.109) | copy-start | bytes 3145732
  275.5 15.7 %collective-permute-start = (bf16[64,32,128]{2,1,0:T(8,128)(2,1)}, bf16[64,32,128]{2,1,0:T(8,128)(2,1)}, u32[]{:S(2)}, u32[]{:S(2)}) collective-permute-start(bf16[64,32,128]{2,1,0:T(8,128)(2,1)} %convert_element_type.51), channel_id=1, source_target_pairs={{0,32},{32,64},{64,96},{96,128},{128,160},{160,192},{192,224},{224... | collective-permute-start | bytes 1572872 | tf_op jit(solution)/shard_map/ppermute | solution.py:22
  278.5 17.5 %collective-permute-start.1 = (bf16[64,32,128]{2,1,0:T(8,128)(2,1)}, bf16[64,32,128]{2,1,0:T(8,128)(2,1)}, u32[]{:S(2)}, u32[]{:S(2)}) collective-permute-start(bf16[64,32,128]{2,1,0:T(8,128)(2,1)} %convert_element_type.51), channel_id=1, source_target_pairs={{32,0},{64,32},{96,64},{128,96},{160,128},{192,160},{224,192},{256... | collective-permute-start | bytes 1572872 | tf_op jit(solution)/shard_map/ppermute | solution.py:23
  300.1 43.7 %all-to-all-start.2 = ((bf16[32,32,256]{2,0,1:T(8,128)(2,1)}), bf16[32,32,256]{2,0,1:T(8,128)(2,1)S(1)}, u32[]{:S(2)}, u32[]{:S(2)}) async-start(bf16[32,32,256]{2,0,1:T(8,128)(2,1)} %copy.103), calls=%async_computation.2 | async-start | bytes 1048576 | tf_op jit(solution)/shard_map/all_to_all | solution.py:81
